TPU v7x, 256 devices: a whole 4x4x8 slice. The times are simulated.
256 devices in a mesh: dp: 64 (over y_hi, z, x), mp: 4 (over y_lo, core).
Axes of the slice: x: 4, y: 4 (y_hi: 2, y_lo: 2; y = y_hi * 2 + y_lo), z: 8, core: 2. Of those that a mesh axis runs over, the one named last changes fastest.
Arguments:
- image_feats: bfloat16 [65536, 1152], P('dp'), may hold values from -16 to 16
- text_feats: bfloat16 [65536, 1152], P('dp'), may hold values from -16 to 16
- image_head: bfloat16 [1152, 1152], P(None, 'mp')
- text_head: bfloat16 [1152, 1152], P(None, 'mp')
- hard_tiles: int32 [512, 16], P('dp'), may hold values from 0 to 511, as said below
- logit_scale: float32 [1], replicated, may hold values from 6 to 16
- logit_bias: float32 [1], replicated, may hold values from -4 to -1
Outputs:
- head_grad_img: float32 [1152, 1152], P('dp', 'mp')
- head_grad_txt: float32 [1152, 1152], P('dp', 'mp')
Inputs may be any that keep to these rules, and one draw needn't show every extreme that they name: `hard_tiles`: row tile g lies in block i = g // 8; with o running over -2 .. -1, 1 .. 2 in order as o_0 .. o_(3), entries 4 * k to 4 * k + 3 of row g are 4 different tiles of block (i + o_k) mod 64, and block j holds tiles 8 * j to 8 * j + 7.
All inputs are finite; a program needn't handle non-finite values.
Results may differ from a plain program's by a relative error of at most 0.0015.
Values may be sent and summed in bfloat16 or wider, within the bound.
No kernel may reach another device: no remote copies, remote signals or barrier semaphores. Data moves between devices by JAX's collectives and lax.ppermute only.
A program may use at most 128 MiB of HBM per device.

v0:
```python
import jax
import jax.numpy as jnp
from jax import lax
from jax.sharding import PartitionSpec as P

EPSILON = 1e-06


def shifted(value, axis, steps):
    count = lax.axis_size(axis)
    pairs = [(source, (source + steps) % count) for source in range(count)]
    return lax.ppermute(value, axis, pairs)


def shards(image_feats, text_feats, image_head, text_head, hard_tiles, logit_scale, logit_bias):
    row_count = image_feats.shape[0]
    width_part = image_head.shape[1]
    per_block = row_count // 128
    model_count = lax.axis_size("mp")
    model_index = lax.axis_index("mp")
    tiles_share = per_block // model_count
    span_blocks = min(2, (lax.axis_size("dp") - 1) // 2)
    pick_count = hard_tiles.shape[1] // (2 * span_blocks)
    temp_scale = logit_scale[0]
    shift_bias = logit_bias[0]
    image_proj = jnp.dot(image_feats, image_head, preferred_element_type=jnp.float32)
    text_proj = jnp.dot(text_feats, text_head, preferred_element_type=jnp.float32)
    norm_img, norm_txt = lax.psum(
        (jnp.sum(image_proj * image_proj, axis=1), jnp.sum(text_proj * text_proj, axis=1)), "mp"
    )
    inverse_img = lax.rsqrt(norm_img + EPSILON)
    inverse_txt = lax.rsqrt(norm_txt + EPSILON)
    image_unit = (image_proj * inverse_img[:, None]).astype(jnp.bfloat16)
    text_unit = (text_proj * inverse_txt[:, None]).astype(jnp.bfloat16)
    image_tiles = image_unit.reshape(per_block, 128, width_part)
    local_ids = hard_tiles % per_block
    image_mine = lax.all_to_all(image_unit, "mp", split_axis=0, concat_axis=1, tiled=True)
    mine_tiles = image_mine.reshape(tiles_share, 128, image_mine.shape[1])
    text_full = lax.all_gather(text_unit, "mp", axis=1, tiled=True)
    partial_value = jnp.dot(image_unit, text_unit.T, preferred_element_type=jnp.float32)
    scores = lax.psum(partial_value, "mp")
    diagonal_mask = jnp.eye(row_count, dtype=jnp.float32)
    weight = (
        temp_scale * (jax.nn.sigmoid(temp_scale * scores + shift_bias) - diagonal_mask)
    ).astype(jnp.bfloat16)
    grad_img = jnp.dot(weight, text_unit, preferred_element_type=jnp.float32)
    grad_txt = jnp.einsum("pq,pe->qe", weight, image_unit, preferred_element_type=jnp.float32)
    current = shifted(text_full, "dp", -span_blocks)
    carried = jnp.zeros_like(text_proj)
    for step_index in range(2 * span_blocks + 1):
        if step_index > 0:
            current = shifted(current, "dp", 1)
            carried = shifted(carried, "dp", 1)
        offset = span_blocks - step_index
        if offset != 0:
            slot_index = offset + span_blocks if offset < 0 else offset + span_blocks - 1
            picked = local_ids[:, pick_count * slot_index : pick_count * slot_index + pick_count]
            picked_mine = lax.dynamic_slice_in_dim(
                picked, model_index * tiles_share, tiles_share, 0
            )
            wide_tiles = current.reshape(per_block, 128, current.shape[1])
            chosen_wide = jnp.take(wide_tiles, picked_mine, axis=0)
            pair_part = jnp.einsum(
                "rpe,rkqe->rkpq", mine_tiles, chosen_wide, preferred_element_type=jnp.float32
            )
            weight_part = (temp_scale * jax.nn.sigmoid(temp_scale * pair_part + shift_bias)).astype(
                jnp.bfloat16
            )
            pair_weight = lax.all_gather(weight_part, "mp", axis=0, tiled=True)
            text_local = lax.dynamic_slice_in_dim(current, model_index * width_part, width_part, 1)
            chosen = jnp.take(text_local.reshape(per_block, 128, width_part), picked, axis=0)
            into_img = jnp.einsum(
                "rkpq,rkqe->rpe", pair_weight, chosen, preferred_element_type=jnp.float32
            )
            into_sel = jnp.einsum(
                "rkpq,rpe->rkqe", pair_weight, image_tiles, preferred_element_type=jnp.float32
            )
            onehot = (
                picked[:, :, None] == jnp.arange(per_block, dtype=jnp.int32)[None, None, :]
            ).astype(jnp.float32)
            into_txt = jnp.einsum(
                "rkt,rkqe->tqe", onehot, into_sel, precision=lax.Precision.HIGHEST
            )
            into_img, into_txt = (
                into_img.reshape(row_count, width_part),
                into_txt.reshape(row_count, width_part),
            )
            grad_img = grad_img + into_img
            carried = carried + into_txt
    grad_txt = grad_txt + shifted(carried, "dp", -span_blocks)
    dots_img, dots_txt = lax.psum(
        (jnp.sum(image_proj * grad_img, axis=1), jnp.sum(text_proj * grad_txt, axis=1)), "mp"
    )
    cube_img = dots_img * inverse_img * inverse_img * inverse_img
    cube_txt = dots_txt * inverse_txt * inverse_txt * inverse_txt
    dproj_img = (inverse_img[:, None] * grad_img - cube_img[:, None] * image_proj).astype(
        jnp.bfloat16
    )
    dproj_txt = (inverse_txt[:, None] * grad_txt - cube_txt[:, None] * text_proj).astype(
        jnp.bfloat16
    )
    local_img = jnp.einsum("nd,ne->de", image_feats, dproj_img, preferred_element_type=jnp.float32)
    local_txt = jnp.einsum("nd,ne->de", text_feats, dproj_txt, preferred_element_type=jnp.float32)
    head_grad_img, head_grad_txt = (
        lax.psum_scatter(local_img, "dp", scatter_dimension=0, tiled=True),
        lax.psum_scatter(local_txt, "dp", scatter_dimension=0, tiled=True),
    )
    return (head_grad_img, head_grad_txt)


def solution(mesh):
    placed = (P("dp", None), P("dp", None), P(None, "mp"), P(None, "mp"), P("dp", None), P(), P())
    return jax.shard_map(
        shards,
        mesh=mesh,
        in_specs=placed,
        out_specs=(P("dp", "mp"), P("dp", "mp")),
        check_vma=False,
    )
```

profile of v0, /device:TPU:24, one launch (start us, length us, event | category | flops | bytes accessed | tf_op | source)
XLA Modules:
  0.0 1375.7 jit_solution(13354665672646321138)
XLA Ops:
  13.0 6.3 all-reduce.4
  20.3 36.2 %all-gather.6.cloned.1.call-done = bf16[1024,1152]{0,1:T(8,128)(2,1)} async-done(((bf16[1024,288]{0,1:T(8,128)(2,1)}), bf16[1024,1152]{0,1:T(8,128)(2,1)}) %all-gather.6.cloned.1.call-update) | async-done | bytes 2359312 | tf_op jit(solution)/shard_map/all_gather | solution.py:39
  56.5 6.3 collective-permute-start
  62.8 51.6 %collective-permute-done = bf16[1024,1152]{0,1:T(8,128)(2,1)} collective-permute-done((bf16[1024,1152]{0,1:T(8,128)(2,1)}, bf16[1024,1152]{0,1:T(8,128)(2,1)}, u32[]{:S(2)}, u32[]{:S(2)}) %collective-permute-start) | collective-permute-done | bytes 2359328 | tf_op jit(solution)/shard_map/ppermute | solution.py:12
  118.1 5.0 all-to-all-start
  128.9 51.7 %all-to-all-done = bf16[4,256,288]{1,2,0:T(8,128)(2,1)} async-done(((bf16[4,256,288]{1,2,0:T(8,128)(2,1)}), bf16[4,256,288]{1,2,0:T(8,128)(2,1)}, u32[]{:S(2)}, u32[]{:S(2)}) %all-to-all-start) | async-done | bytes 589856 | tf_op jit(solution)/shard_map/all_to_all | solution.py:37
  186.0 4.3 copy.141
  203.4 4.3 copy.144
  216.9 4.5 fusion.197
  221.5 40.0 %collective-permute-done.2 = bf16[1024,1152]{0,1:T(8,128)(2,1)} collective-permute-done((bf16[1024,1152]{0,1:T(8,128)(2,1)}, bf16[1024,1152]{0,1:T(8,128)(2,1)}, u32[]{:S(2)}, u32[]{:S(2)}) %collective-permute-start.2) | collective-permute-done | bytes 2359328 | tf_op jit(solution)/shard_map/ppermute | solution.py:12
  284.2 6.1 fusion.6
  293.4 28.5 %collective-permute-done.3 = bf16[1024,1152]{0,1:T(8,128)(2,1)} collective-permute-done((bf16[1024,1152]{0,1:T(8,128)(2,1)}, bf16[1024,1152]{0,1:T(8,128)(2,1)}, u32[]{:S(2)}, u32[]{:S(2)}) %collective-permute-start.3) | collective-permute-done | bytes 2359328 | tf_op jit(solution)/shard_map/ppermute | solution.py:12
  322.1 80.4 %all-gather.10.cloned.1.call-done = bf16[8,4,128,128]{3,2,1,0:T(8,128)(2,1)} async-done(((bf16[2,4,128,128]{3,2,1,0:T(8,128)(2,1)}), bf16[8,4,128,128]{3,2,1,0:T(8,128)(2,1)}) %all-gather.10.cloned.1.call-update) | async-done | bytes 1048592 | tf_op jit(solution)/shard_map/all_gather | solution.py:69
  404.7 6.1 fusion.4
  427.2 85.8 %all-reduce.8.cloned.1.call-done = f32[1024,1024]{1,0:T(8,128)} async-done(((f32[1024,1024]{1,0:T(8,128)}), f32[1024,1024]{1,0:T(8,128)}) %all-reduce.8.cloned.1.call-update) | async-done | bytes 4194320 | tf_op jit(solution)/shard_map/psum | solution.py:41
  513.0 4.7 multiply_convert_fusion
  528.8 4.4 copy.150
  547.8 16.5 %all-gather.12.cloned.1.call-done = bf16[8,4,128,128]{3,2,1,0:T(8,128)(2,1)} async-done(((bf16[2,4,128,128]{3,2,1,0:T(8,128)(2,1)}), bf16[8,4,128,128]{3,2,1,0:T(8,128)(2,1)}) %all-gather.12.cloned.1.call-update) | async-done | bytes 1048592 | tf_op jit(solution)/shard_map/all_gather | solution.py:69
  566.5 6.1 fusion.2
  585.0 6.1 fusion
  591.2 36.0 %collective-permute-done.8 = f32[1024,288]{0,1:T(8,128)} collective-permute-done((f32[1024,288]{0,1:T(8,128)}, f32[1024,288]{0,1:T(8,128)}, u32[]{:S(2)}, u32[]{:S(2)}) %collective-permute-start.8) | collective-permute-done | bytes 1179680 | tf_op jit(solution)/shard_map/ppermute | solution.py:12
  644.5 14.9 %collective-permute-done.9 = f32[1024,288]{0,1:T(8,128)} collective-permute-done((f32[1024,288]{0,1:T(8,128)}, f32[1024,288]{0,1:T(8,128)}, u32[]{:S(2)}, u32[]{:S(2)}) %collective-permute-start.9) | collective-permute-done | bytes 1179680 | tf_op jit(solution)/shard_map/ppermute | solution.py:12
  662.6 6.7 all-reduce.3
  679.2 685.8 %all-reduce.10.cloned.1.call-done = (f32[1152,288]{0,1:T(8,128)}, f32[1152,288]{0,1:T(8,128)}) async-done(((f32[1152,288]{0,1:T(8,128)}, f32[1152,288]{0,1:T(8,128)}), (f32[1152,288]{0,1:T(8,128)}, f32[1152,288]{0,1:T(8,128)})) %all-reduce.10.cloned.1.call-update) | async-done | bytes 2654224
  (179 shorter events, 160.7 us)
Async XLA Ops:
  7.2 49.3 %all-gather.6.cloned.1.call-start = ((), (), s32[]{:S(2)}) async-start(), calls=%async_computation.2 | async-start | bytes 2949120 | tf_op jit(solution)/shard_map/all_gather | solution.py:39
  19.3 43.5 %copy-start.16 = (f32[1024]{0:T(1024)}, f32[1024]{0:T(1024)S(1)}, u32[]{:S(2)}) copy-start(f32[1024]{0:T(1024)S(1)} %get-tuple-element.17) | copy-start | bytes 12292
  19.3 98.8 %copy-start.15 = (f32[1024]{0:T(1024)}, f32[1024]{0:T(1024)S(1)}, u32[]{:S(2)}) copy-start(f32[1024]{0:T(1024)S(1)} %get-tuple-element.16) | copy-start | bytes 12292
  20.3 104.1 %copy-start.24 = (s32[8,16]{1,0:T(8,128)S(1)}, s32[8,16]{1,0:T(8,128)}, u32[]{:S(2)}) copy-start(s32[8,16]{1,0:T(8,128)} %param.15) | copy-start | bytes 1540
  56.5 57.9 %collective-permute-start = (bf16[1024,1152]{0,1:T(8,128)(2,1)}, bf16[1024,1152]{0,1:T(8,128)(2,1)}, u32[]{:S(2)}, u32[]{:S(2)}) collective-permute-start(bf16[1024,1152]{0,1:T(8,128)(2,1)} %all-gather.6.cloned.1.call-done), channel_id=1, source_target_pairs={{0,248},{4,252},{8,0},{12,4},{16,8},{20,12},{24,16},{28,20},{32,24... | collective-permute-start | bytes 7077896 | tf_op jit(solution)/shard_map/ppermute | solution.py:12
  114.4 87.7 %collective-permute-start.1 = (bf16[1024,1152]{0,1:T(8,128)(2,1)}, bf16[1024,1152]{0,1:T(8,128)(2,1)}, u32[]{:S(2)}, u32[]{:S(2)}) collective-permute-start(bf16[1024,1152]{0,1:T(8,128)(2,1)} %collective-permute-done), channel_id=1, source_target_pairs={{0,4},{4,8},{8,12},{12,16},{16,20},{20,24},{24,28},{28,32},{32,36}... | collective-permute-start | bytes 7077896 | tf_op jit(solution)/shard_map/ppermute | solution.py:12
  118.1 62.4 %all-to-all-start = ((bf16[4,256,288]{1,2,0:T(8,128)(2,1)}), bf16[4,256,288]{1,2,0:T(8,128)(2,1)}, u32[]{:S(2)}, u32[]{:S(2)}) async-start(bf16[4,256,288]{1,2,0:T(8,128)(2,1)} %bitcast.192), calls=%async_computation | async-start | bytes 1179648 | tf_op jit(solution)/shard_map/all_to_all | solution.py:37
  123.1 158.9 %all-gather.8.cloned.1.call-start = ((), (), s32[]{:S(2)}) async-start(), calls=%async_computation.3 | async-start | bytes 1310720 | tf_op jit(solution)/shard_map/all_gather | solution.py:69
  199.5 203.1 %all-gather.10.cloned.1.call-start = ((), (), s32[]{:S(2)}) async-start(), calls=%async_computation.4 | async-start | bytes 1310720 | tf_op jit(solution)/shard_map/all_gather | solution.py:69
  202.1 59.4 %collective-permute-start.2 = (bf16[1024,1152]{0,1:T(8,128)(2,1)}, bf16[1024,1152]{0,1:T(8,128)(2,1)}, u32[]{:S(2)}, u32[]{:S(2)}) collective-permute-start(bf16[1024,1152]{0,1:T(8,128)(2,1)} %collective-permute-done.1), channel_id=1, source_target_pairs={{0,4},{4,8},{8,12},{12,16},{16,20},{20,24},{24,28},{28,32},{32,36}... | collective-permute-start | bytes 7077896 | tf_op jit(solution)/shard_map/ppermute | solution.py:12
  216.9 296.2 %all-reduce.8.cloned.1.call-start = ((), (), s32[]{:S(2)}) async-start(), calls=%async_computation.1 | async-start | bytes 8388608 | tf_op jit(solution)/shard_map/psum | solution.py:41
  221.5 342.8 %all-gather.12.cloned.1.call-start = ((), (), s32[]{:S(2)}) async-start(), calls=%async_computation.5 | async-start | bytes 1310720 | tf_op jit(solution)/shard_map/all_gather | solution.py:69
  261.5 60.4 %collective-permute-start.3 = (bf16[1024,1152]{0,1:T(8,128)(2,1)}, bf16[1024,1152]{0,1:T(8,128)(2,1)}, u32[]{:S(2)}, u32[]{:S(2)}) collective-permute-start(bf16[1024,1152]{0,1:T(8,128)(2,1)} %collective-permute-done.2), channel_id=1, source_target_pairs={{0,4},{4,8},{8,12},{12,16},{16,20},{20,24},{24,28},{28,32},{32,36}... | collective-permute-start | bytes 7077896 | tf_op jit(solution)/shard_map/ppermute | solution.py:12
  291.6 119.2 %collective-permute-start.5 = (f32[1024,288]{0,1:T(8,128)}, f32[1024,288]{0,1:T(8,128)}, u32[]{:S(2)}, u32[]{:S(2)}) collective-permute-start(f32[1024,288]{0,1:T(8,128)} %bitcast.159), channel_id=1, source_target_pairs={{0,4},{4,8},{8,12},{12,16},{16,20},{20,24},{24,28},{28,32},{32,36}... | collective-permute-start | bytes 3538952 | tf_op jit(solution)/shard_map/ppermute | solution.py:12
  293.4 111.3 %copy-start.22 = (s32[8,4]{0,1:T(4,128)S(1)}, s32[8,4]{0,1:T(4,128)}, u32[]{:S(2)}) copy-start(s32[8,4]{0,1:T(4,128)} %copy.114) | copy-start | bytes 388
  321.9 206.9 %collective-permute-start.4 = (bf16[1024,1152]{0,1:T(8,128)(2,1)}, bf16[1024,1152]{0,1:T(8,128)(2,1)}, u32[]{:S(2)}, u32[]{:S(2)}) collective-permute-start(bf16[1024,1152]{0,1:T(8,128)(2,1)} %collective-permute-done.3), channel_id=1, source_target_pairs={{0,4},{4,8},{8,12},{12,16},{16,20},{20,24},{24,28},{28,32},{32,36}... | collective-permute-start | bytes 7077896 | tf_op jit(solution)/shard_map/ppermute | solution.py:12
  413.7 113.3 %collective-permute-start.6 = (f32[1024,288]{0,1:T(8,128)}, f32[1024,288]{0,1:T(8,128)}, u32[]{:S(2)}, u32[]{:S(2)}) collective-permute-start(f32[1024,288]{0,1:T(8,128)} %bitcast_add_fusion.2), channel_id=1, source_target_pairs={{0,4},{4,8},{8,12},{12,16},{16,20},{20,24},{24,28},{28,32},{32,36}... | collective-permute-start | bytes 3538952 | tf_op jit(solution)/shard_map/ppermute | solution.py:12
  427.2 155.7 %all-gather.14.cloned.1.call-start = ((), (), s32[]{:S(2)}) async-start(), calls=%async_computation.6 | async-start | bytes 1310720 | tf_op jit(solution)/shard_map/all_gather | solution.py:69
  527.0 45.7 %collective-permute-start.7 = (f32[1024,288]{0,1:T(8,128)}, f32[1024,288]{0,1:T(8,128)}, u32[]{:S(2)}, u32[]{:S(2)}) collective-permute-start(f32[1024,288]{0,1:T(8,128)} %collective-permute-done.6), channel_id=1, source_target_pairs={{0,4},{4,8},{8,12},{12,16},{16,20},{20,24},{24,28},{28,32},{32,36}... | collective-permute-start | bytes 3538952 | tf_op jit(solution)/shard_map/ppermute | solution.py:12
  542.5 822.5 %all-reduce.10.cloned.1.call-start = ((), (), s32[]{:S(2)}) async-start(), calls=%async_computation.7 | async-start | bytes 5308416
  575.5 51.7 %collective-permute-start.8 = (f32[1024,288]{0,1:T(8,128)}, f32[1024,288]{0,1:T(8,128)}, u32[]{:S(2)}, u32[]{:S(2)}) collective-permute-start(f32[1024,288]{0,1:T(8,128)} %bitcast_add_fusion.1), channel_id=1, source_target_pairs={{0,4},{4,8},{8,12},{12,16},{16,20},{20,24},{24,28},{28,32},{32,36}... | collective-permute-start | bytes 3538952 | tf_op jit(solution)/shard_map/ppermute | solution.py:12
  591.2 38.9 %copy-start.13 = (bf16[8,4,128,128]{3,2,1,0:T(8,128)(2,1)S(1)}, bf16[8,4,128,128]{3,2,1,0:T(8,128)(2,1)}, u32[]{:S(2)}) copy-start(bf16[8,4,128,128]{3,2,1,0:T(8,128)(2,1)} %all-gather.12.cloned.1.call-done) | copy-start | bytes 3145732
  591.2 38.9 %copy-start.28 = (pred[8,4]{1,0:T(8,128)(4,1)S(1)}, pred[8,4]{1,0:T(8,128)(4,1)}, u32[]{:S(2)}) copy-start(pred[8,4]{1,0:T(8,128)(4,1)} %get-tuple-element.28) | copy-start | bytes 100
  629.9 29.6 %collective-permute-start.9 = (f32[1024,288]{0,1:T(8,128)}, f32[1024,288]{0,1:T(8,128)}, u32[]{:S(2)}, u32[]{:S(2)}) collective-permute-start(f32[1024,288]{0,1:T(8,128)} %bitcast_add_fusion), channel_id=1, source_target_pairs={{0,248},{4,252},{8,0},{12,4},{16,8},{20,12},{24,16},{28,20},{32,24... | collective-permute-start | bytes 3538952 | tf_op jit(solution)/shard_map/ppermute | solution.py:12
  (28 other events, 153.3 us)
Sparse Core Ops, SparseCore 0:
  20.4 36.0 all-gather.5
  199.6 66.6 all-gather.7
  268.1 134.4 all-gather.9
  405.0 107.9 all-reduce.7
  514.7 49.5 all-gather.11
  566.0 16.3 all-gather.13
  677.5 687.4 all-reduce.9
where the time goes:
time: 1390 us; the launch traced here: 1380 us
  waiting for transfers between devices  1130 us (81%)
  local copies, waits for them, and re-layouts  94.1 us (7%)
  matrix products  79.9 us (6%)
  other arithmetic  29.9 us (2%)
  between operations  16.7 us (1%)
  starting transfers between devices  14.7 us (1%)
    unnamed x8, waiting for transfers between devices  686 us
    ppermute x10, waiting for transfers between devices, shifted(): return lax.ppermute(value, axis, pairs)  171 us
    all_gather x4, waiting for transfers between devices, shards(): pair_weight = lax.all_gather(weight_part, 'mp', axis=0, tiled=True)  96.9 us
    psum x1, waiting for transfers between devices, shards(): scores = lax.psum(partial_value, 'mp')  85.8 us
    all_to_all x1, waiting for transfers between devices, shards(): lax.all_to_all(image_unit, 'mp', split_axis=0, concat_axis=1, tiled=True)  51.7 us
    all_gather x1, waiting for transfers between devices, shards(): text_full = lax.all_gather(text_unit, 'mp', axis=1, tiled=True)  36.2 us
  transfers between devices with their start and end apart: 18, of which 11 were waited for; matrix products, arithmetic and copies ran while one was open for 13% of the time, Pallas kernels for 0%

commit v1 on v0

--- a/solution.py
+++ b/solution.py
@@ -38,7 +38,7 @@
     mine_tiles = image_mine.reshape(tiles_share, 128, image_mine.shape[1])
     text_full = lax.all_gather(text_unit, "mp", axis=1, tiled=True)
     partial_value = jnp.dot(image_unit, text_unit.T, preferred_element_type=jnp.float32)
-    scores = lax.psum(partial_value, "mp")
+    scores = jnp.sum(jax.lax.all_gather(partial_value, axis_name="mp"), 0)
     diagonal_mask = jnp.eye(row_count, dtype=jnp.float32)
     weight = (
         temp_scale * (jax.nn.sigmoid(temp_scale * scores + shift_bias) - diagonal_mask)

time: 1390 us -> 1410 us (1.014)
    all_gather x0 -> x1, waiting for transfers between devices: none -> 110 us  [shards(): scores = jnp.sum(jax.lax.all_gather(partial_value, axis_name='mp'), 0)]
    all_gather x4, waiting for transfers between devices: 96.9 us -> 0.01 us  [shards(): pair_weight = lax.all_gather(weight_part, 'mp', axis=0, tiled=True)]
    psum x1 -> x0, waiting for transfers between devices: 85.8 us -> none  [shards(): scores = lax.psum(partial_value, 'mp')]
    ppermute x10, waiting for transfers between devices: 171 us -> 245 us  [shifted(): return lax.ppermute(value, axis, pairs)]
  transfers between devices with their start and end apart: 18 -> 18, of which waited for: 11 -> 12; matrix products, arithmetic and copies ran while one was open for 13% -> 14% of each run, Pallas kernels for 0% -> 0%
where the time goes in v1:
time: 1410 us; the launch traced here: 1400 us
  waiting for transfers between devices  1140 us (81%)
  local copies, waits for them, and re-layouts  95.4 us (7%)
  matrix products  80.6 us (6%)
  other arithmetic  39.9 us (3%)
  between operations  16.9 us (1%)
  blocking collectives  14.7 us (1%)
    unnamed x8, waiting for transfers between devices  697 us
    ppermute x10, waiting for transfers between devices, shifted(): return lax.ppermute(value, axis, pairs)  245 us
    all_gather x1, waiting for transfers between devices, shards(): scores = jnp.sum(jax.lax.all_gather(partial_value, axis_name='mp'), 0)  110 us
    all_to_all x1, waiting for transfers between devices, shards(): lax.all_to_all(image_unit, 'mp', split_axis=0, concat_axis=1, tiled=True)  51 us
    all_gather x1, waiting for transfers between devices, shards(): text_full = lax.all_gather(text_unit, 'mp', axis=1, tiled=True)  36.2 us
  transfers between devices with their start and end apart: 18, of which 12 were waited for; matrix products, arithmetic and copies ran while one was open for 14% of the time, Pallas kernels for 0%

profile of v1, /device:TPU:24, one launch (start us, length us, event | category | flops | bytes accessed | tf_op | source)
XLA Modules:
  0.0 1400.8 jit_solution(6495815879669699268)
XLA Ops:
  13.0 6.3 all-reduce.4
  20.3 36.2 %all-gather.8.cloned.1.call-done = bf16[1024,1152]{0,1:T(8,128)(2,1)} async-done(((bf16[1024,288]{0,1:T(8,128)(2,1)}), bf16[1024,1152]{0,1:T(8,128)(2,1)}) %all-gather.8.cloned.1.call-update) | async-done | bytes 2359312 | tf_op jit(solution)/shard_map/all_gather | solution.py:39
  56.5 6.3 collective-permute-start
  62.8 51.6 %collective-permute-done = bf16[1024,1152]{0,1:T(8,128)(2,1)S(1)} collective-permute-done((bf16[1024,1152]{0,1:T(8,128)(2,1)}, bf16[1024,1152]{0,1:T(8,128)(2,1)S(1)}, u32[]{:S(2)}, u32[]{:S(2)}) %collective-permute-start) | collective-permute-done | bytes 2359328 | tf_op jit(solution)/shard_map/ppermute | solution.py:12
  116.5 58.8 %collective-permute-done.1 = bf16[1024,1152]{0,1:T(8,128)(2,1)} collective-permute-done((bf16[1024,1152]{0,1:T(8,128)(2,1)S(1)}, bf16[1024,1152]{0,1:T(8,128)(2,1)}, u32[]{:S(2)}, u32[]{:S(2)}) %collective-permute-start.1) | collective-permute-done | bytes 2359328 | tf_op jit(solution)/shard_map/ppermute | solution.py:12
  178.4 5.0 all-to-all-start
  189.1 51.0 %all-to-all-done = bf16[4,256,288]{1,2,0:T(8,128)(2,1)} async-done(((bf16[4,256,288]{1,2,0:T(8,128)(2,1)}), bf16[4,256,288]{1,2,0:T(8,128)(2,1)}, u32[]{:S(2)}, u32[]{:S(2)}) %all-to-all-start) | async-done | bytes 589856 | tf_op jit(solution)/shard_map/all_to_all | solution.py:37
  276.5 25.5 %collective-permute-done.3 = bf16[1024,1152]{0,1:T(8,128)(2,1)} collective-permute-done((bf16[1024,1152]{0,1:T(8,128)(2,1)}, bf16[1024,1152]{0,1:T(8,128)(2,1)}, u32[]{:S(2)}, u32[]{:S(2)}) %collective-permute-start.3) | collective-permute-done | bytes 2359328 | tf_op jit(solution)/shard_map/ppermute | solution.py:12
  305.0 4.4 copy.147
  322.6 37.8 %collective-permute-done.4 = bf16[1024,1152]{0,1:T(8,128)(2,1)} collective-permute-done((bf16[1024,1152]{0,1:T(8,128)(2,1)}, bf16[1024,1152]{0,1:T(8,128)(2,1)}, u32[]{:S(2)}, u32[]{:S(2)}) %collective-permute-start.4) | collective-permute-done | bytes 2359328 | tf_op jit(solution)/shard_map/ppermute | solution.py:12
  360.4 4.4 copy.150
  374.0 4.5 fusion.197
  384.5 6.1 fusion.6
  397.0 6.1 fusion.4
  403.1 21.4 %collective-permute-done.5 = f32[1024,288]{0,1:T(8,128)} collective-permute-done((f32[1024,288]{0,1:T(8,128)}, f32[1024,288]{0,1:T(8,128)}, u32[]{:S(2)}, u32[]{:S(2)}) %collective-permute-start.5) | collective-permute-done | bytes 1179680 | tf_op jit(solution)/shard_map/ppermute | solution.py:12
  452.1 6.3 collective-permute-done.6
  470.0 6.1 fusion.2
  476.2 12.8 collective-permute-done.7
  501.6 6.1 fusion
  507.7 30.8 %collective-permute-done.8 = f32[1024,288]{0,1:T(8,128)} collective-permute-done((f32[1024,288]{0,1:T(8,128)}, f32[1024,288]{0,1:T(8,128)}, u32[]{:S(2)}, u32[]{:S(2)}) %collective-permute-start.8) | collective-permute-done | bytes 1179680 | tf_op jit(solution)/shard_map/ppermute | solution.py:12
  543.4 110.3 %all-gather.18.cloned.1.call-done = f32[4096,1024]{1,0:T(8,128)} async-done(((f32[1024,1024]{1,0:T(8,128)}), f32[4096,1024]{1,0:T(8,128)}) %all-gather.18.cloned.1.call-update) | async-done | bytes 16777232 | tf_op jit(solution)/shard_map/all_gather | solution.py:41
  653.6 10.3 reduce_sum.47
  674.2 8.4 all-reduce.3
  692.6 697.3 %all-reduce.7.cloned.1.call-done = (f32[1152,288]{0,1:T(8,128)}, f32[1152,288]{0,1:T(8,128)}) async-done(((f32[1152,288]{0,1:T(8,128)}, f32[1152,288]{0,1:T(8,128)}), (f32[1152,288]{0,1:T(8,128)}, f32[1152,288]{0,1:T(8,128)})) %all-reduce.7.cloned.1.call-update) | async-done | bytes 2654224
  (174 shorter events, 169.9 us)
Async XLA Ops:
  7.2 49.3 %all-gather.8.cloned.1.call-start = ((), (), s32[]{:S(2)}) async-start(), calls=%async_computation.1 | async-start | bytes 2949120 | tf_op jit(solution)/shard_map/all_gather | solution.py:39
  19.3 156.0 %copy-start.18 = (f32[1024]{0:T(1024)}, f32[1024]{0:T(1024)S(1)}, u32[]{:S(2)}) copy-start(f32[1024]{0:T(1024)S(1)} %get-tuple-element.17) | copy-start | bytes 12292
  19.3 159.1 %copy-start.17 = (f32[1024]{0:T(1024)}, f32[1024]{0:T(1024)S(1)}, u32[]{:S(2)}) copy-start(f32[1024]{0:T(1024)S(1)} %get-tuple-element.16) | copy-start | bytes 12292
  20.3 164.5 %copy-start.25 = (s32[8,16]{1,0:T(8,128)S(1)}, s32[8,16]{1,0:T(8,128)}, u32[]{:S(2)}) copy-start(s32[8,16]{1,0:T(8,128)} %param.15) | copy-start | bytes 1540
  56.5 57.9 %collective-permute-start = (bf16[1024,1152]{0,1:T(8,128)(2,1)}, bf16[1024,1152]{0,1:T(8,128)(2,1)S(1)}, u32[]{:S(2)}, u32[]{:S(2)}) collective-permute-start(bf16[1024,1152]{0,1:T(8,128)(2,1)} %all-gather.8.cloned.1.call-done), channel_id=1, source_target_pairs={{0,248},{4,252},{8,0},{12,4},{16,8},{20,12},{24,16},{28,20},{32,24... | collective-permute-start | bytes 7077896 | tf_op jit(solution)/shard_map/ppermute | solution.py:12
  115.9 59.4 %collective-permute-start.1 = (bf16[1024,1152]{0,1:T(8,128)(2,1)S(1)}, bf16[1024,1152]{0,1:T(8,128)(2,1)}, u32[]{:S(2)}, u32[]{:S(2)}) collective-permute-start(bf16[1024,1152]{0,1:T(8,128)(2,1)S(1)} %collective-permute-done), channel_id=1, source_target_pairs={{0,4},{4,8},{8,12},{12,16},{16,20},{20,24},{24,28},{28,32},{32,36}... | collective-permute-start | bytes 7077896 | tf_op jit(solution)/shard_map/ppermute | solution.py:12
  175.3 67.3 %collective-permute-start.2 = (bf16[1024,1152]{0,1:T(8,128)(2,1)}, bf16[1024,1152]{0,1:T(8,128)(2,1)}, u32[]{:S(2)}, u32[]{:S(2)}) collective-permute-start(bf16[1024,1152]{0,1:T(8,128)(2,1)} %collective-permute-done.1), channel_id=1, source_target_pairs={{0,4},{4,8},{8,12},{12,16},{16,20},{20,24},{24,28},{28,32},{32,36}... | collective-permute-start | bytes 7077896 | tf_op jit(solution)/shard_map/ppermute | solution.py:12
  178.4 61.7 %all-to-all-start = ((bf16[4,256,288]{1,2,0:T(8,128)(2,1)}), bf16[4,256,288]{1,2,0:T(8,128)(2,1)}, u32[]{:S(2)}, u32[]{:S(2)}) async-start(bf16[4,256,288]{1,2,0:T(8,128)(2,1)} %bitcast.194), calls=%async_computation | async-start | bytes 1179648 | tf_op jit(solution)/shard_map/all_to_all | solution.py:37
  183.4 198.8 %all-gather.10.cloned.1.call-start = ((), (), s32[]{:S(2)}) async-start(), calls=%async_computation.2 | async-start | bytes 1310720 | tf_op jit(solution)/shard_map/all_gather | solution.py:69
  242.6 59.4 %collective-permute-start.3 = (bf16[1024,1152]{0,1:T(8,128)(2,1)}, bf16[1024,1152]{0,1:T(8,128)(2,1)}, u32[]{:S(2)}, u32[]{:S(2)}) collective-permute-start(bf16[1024,1152]{0,1:T(8,128)(2,1)} %collective-permute-done.2), channel_id=1, source_target_pairs={{0,4},{4,8},{8,12},{12,16},{16,20},{20,24},{24,28},{28,32},{32,36}... | collective-permute-start | bytes 7077896 | tf_op jit(solution)/shard_map/ppermute | solution.py:12
  259.1 135.7 %all-gather.12.cloned.1.call-start = ((), (), s32[]{:S(2)}) async-start(), calls=%async_computation.3 | async-start | bytes 1310720 | tf_op jit(solution)/shard_map/all_gather | solution.py:69
  276.4 191.5 %all-gather.14.cloned.1.call-start = ((), (), s32[]{:S(2)}) async-start(), calls=%async_computation.4 | async-start | bytes 1310720 | tf_op jit(solution)/shard_map/all_gather | solution.py:69
  302.0 58.4 %collective-permute-start.4 = (bf16[1024,1152]{0,1:T(8,128)(2,1)}, bf16[1024,1152]{0,1:T(8,128)(2,1)}, u32[]{:S(2)}, u32[]{:S(2)}) collective-permute-start(bf16[1024,1152]{0,1:T(8,128)(2,1)} %collective-permute-done.3), channel_id=1, source_target_pairs={{0,4},{4,8},{8,12},{12,16},{16,20},{20,24},{24,28},{28,32},{32,36}... | collective-permute-start | bytes 7077896 | tf_op jit(solution)/shard_map/ppermute | solution.py:12
  318.5 180.7 %all-gather.16.cloned.1.call-start = ((), (), s32[]{:S(2)}) async-start(), calls=%async_computation.5 | async-start | bytes 1310720 | tf_op jit(solution)/shard_map/all_gather | solution.py:69
  373.9 279.7 %all-gather.18.cloned.1.call-start = ((), (), s32[]{:S(2)}) async-start(), calls=%async_computation.6 | async-start | bytes 20971520 | tf_op jit(solution)/shard_map/all_gather | solution.py:41
  378.6 1011.3 %all-reduce.7.cloned.1.call-start = ((), (), s32[]{:S(2)}) async-start(), calls=%async_computation.7 | async-start | bytes 5308416
  391.8 32.7 %collective-permute-start.5 = (f32[1024,288]{0,1:T(8,128)}, f32[1024,288]{0,1:T(8,128)}, u32[]{:S(2)}, u32[]{:S(2)}) collective-permute-start(f32[1024,288]{0,1:T(8,128)} %bitcast.160), channel_id=1, source_target_pairs={{0,4},{4,8},{8,12},{12,16},{16,20},{20,24},{24,28},{28,32},{32,36}... | collective-permute-start | bytes 3538952 | tf_op jit(solution)/shard_map/ppermute | solution.py:12
  427.1 31.3 %collective-permute-start.6 = (f32[1024,288]{0,1:T(8,128)}, f32[1024,288]{0,1:T(8,128)}, u32[]{:S(2)}, u32[]{:S(2)}) collective-permute-start(f32[1024,288]{0,1:T(8,128)} %bitcast_add_fusion.2), channel_id=1, source_target_pairs={{0,4},{4,8},{8,12},{12,16},{16,20},{20,24},{24,28},{28,32},{32,36}... | collective-permute-start | bytes 3538952 | tf_op jit(solution)/shard_map/ppermute | solution.py:12
  458.5 30.5 %collective-permute-start.7 = (f32[1024,288]{0,1:T(8,128)}, f32[1024,288]{0,1:T(8,128)}, u32[]{:S(2)}, u32[]{:S(2)}) collective-permute-start(f32[1024,288]{0,1:T(8,128)} %collective-permute-done.6), channel_id=1, source_target_pairs={{0,4},{4,8},{8,12},{12,16},{16,20},{20,24},{24,28},{28,32},{32,36}... | collective-permute-start | bytes 3538952 | tf_op jit(solution)/shard_map/ppermute | solution.py:12
  491.7 46.9 %collective-permute-start.8 = (f32[1024,288]{0,1:T(8,128)}, f32[1024,288]{0,1:T(8,128)}, u32[]{:S(2)}, u32[]{:S(2)}) collective-permute-start(f32[1024,288]{0,1:T(8,128)} %bitcast_add_fusion.1), channel_id=1, source_target_pairs={{0,4},{4,8},{8,12},{12,16},{16,20},{20,24},{24,28},{28,32},{32,36}... | collective-permute-start | bytes 3538952 | tf_op jit(solution)/shard_map/ppermute | solution.py:12
  507.7 33.7 %copy-start.6 = (bf16[32,128,288]{1,2,0:T(8,128)(2,1)S(1)}, bf16[32,128,288]{1,2,0:T(8,128)(2,1)}, u32[]{:S(2)}) copy-start(bf16[32,128,288]{1,2,0:T(8,128)(2,1)} %gather_fusion.7) | copy-start | bytes 7077892
  507.7 33.7 %copy-start.15 = (bf16[8,4,128,128]{3,2,1,0:T(8,128)(2,1)S(1)}, bf16[8,4,128,128]{3,2,1,0:T(8,128)(2,1)}, u32[]{:S(2)}) copy-start(bf16[8,4,128,128]{3,2,1,0:T(8,128)(2,1)} %all-gather.16.cloned.1.call-done) | copy-start | bytes 3145732
  507.7 33.8 %copy-start.27 = (pred[8,4]{1,0:T(8,128)(4,1)S(1)}, pred[8,4]{1,0:T(8,128)(4,1)}, u32[]{:S(2)}) copy-start(pred[8,4]{1,0:T(8,128)(4,1)} %get-tuple-element.27) | copy-start | bytes 100
  541.2 129.9 %collective-permute-start.9 = (f32[1024,288]{0,1:T(8,128)}, f32[1024,288]{0,1:T(8,128)}, u32[]{:S(2)}, u32[]{:S(2)}) collective-permute-start(f32[1024,288]{0,1:T(8,128)} %bitcast_add_fusion), channel_id=1, source_target_pairs={{0,248},{4,252},{8,0},{12,4},{16,8},{20,12},{24,16},{28,20},{32,24... | collective-permute-start | bytes 3538952 | tf_op jit(solution)/shard_map/ppermute | solution.py:12
  (25 other events, 130.5 us)
Sparse Core Ops, SparseCore 0:
  20.4 36.0 all-gather.7
  259.2 99.9 all-gather.9
  361.1 16.9 all-gather.11
  379.8 49.4 all-gather.13
  430.9 59.6 all-gather.15
  492.2 161.3 all-gather.17
  690.8 698.9 all-reduce.6
